TPU v7x, 32 devices: a whole 2x2x4 slice. The times are simulated.
32 devices in a mesh: grp: 2 (over x), gx: 16 (over z, y, core).
Axes of the slice: x: 2, y: 2, z: 4, core: 2. Of those that a mesh axis runs over, the one named last changes fastest.
Arguments:
- e_forward: float32 [3, 256, 32, 256], P(None, ('grp', 'gx')), parts along dimension 1, may hold values from -6 to 6
- h_forward: float32 [3, 256, 32, 256], P(None, ('grp', 'gx')), parts along dimension 1, may hold values from -6 to 6
- p_forward: float32 [3, 256, 32, 256], P(None, ('grp', 'gx')), parts along dimension 1, may hold values from -6 to 6
- j_forward: float32 [3, 256, 32, 256], P(None, ('grp', 'gx')), parts along dimension 1, may hold values from -6 to 6
- e_adjoint: float32 [3, 256, 32, 256], P(None, ('grp', 'gx')), parts along dimension 1, may hold values from -6 to 6
- h_adjoint: float32 [3, 256, 32, 256], P(None, ('grp', 'gx')), parts along dimension 1, may hold values from -6 to 6
- p_adjoint: float32 [3, 256, 32, 256], P(None, ('grp', 'gx')), parts along dimension 1, may hold values from -6 to 6
- j_adjoint: float32 [3, 256, 32, 256], P(None, ('grp', 'gx')), parts along dimension 1, may hold values from -6 to 6
- design: float32 [32, 32, 256], P(('grp', 'gx')), parts along dimension 0, may hold values from 0 to 1
- source_amp: float32 [32, 3], P('grp'), parts along dimension 0, may hold values from -6 to 6
- source_cell: int32 [32], P('grp'), parts along dimension 0, may hold values from 0 to 1048575
- monitor_cell: int32 [32], P('grp'), parts along dimension 0, may hold values from 0 to 1048575
- slab_start: int32 [2], P('grp'), parts along dimension 0, may hold values from 8 to 15
- radius: int32 [2], P('grp'), parts along dimension 0, may hold values from 1 to 4
Outputs:
- e_forward_next: float32 [3, 256, 32, 256], P(None, ('grp', 'gx')), parts along dimension 1
- h_forward_next: float32 [3, 256, 32, 256], P(None, ('grp', 'gx')), parts along dimension 1
- e_adjoint_next: float32 [3, 256, 32, 256], P(None, ('grp', 'gx')), parts along dimension 1
- h_adjoint_next: float32 [3, 256, 32, 256], P(None, ('grp', 'gx')), parts along dimension 1
- design_grad: float32 [32, 32, 256], P(('grp', 'gx')), parts along dimension 0
There are 2 independent parts, one for each index of `grp`. A program takes and returns all parts, laid end to end along the dimension named above; each array names one. Nothing has to cross between parts.
Inputs may be any that keep to these rules, and one draw needn't show every extreme that they name: `slab_start`: the slab begins within planes 8 to 15 of the grid.
All inputs are finite; a program needn't handle non-finite values.
Results may differ from a plain program's by a relative error of at most 0.0003.
Values sent between devices are 32-bit elements; how exact they have to be, the bound alone decides.
No kernel may reach another device: no remote copies, remote signals or barrier semaphores. Data moves between devices by JAX's collectives and lax.ppermute only.
A program may use at most 128 MiB of HBM per device.

v0:
```python
import jax
import jax.numpy as jnp
from jax import lax
from jax.sharding import PartitionSpec as P

DT = 0.5
EPS_RANGE = 10.0
STRENGTH_BASE = 0.5
STRENGTH_RANGE = 3.0
DAMPING = 0.2
GAIN_FIELD = 0.25
HIGH = lax.Precision.HIGHEST


def passed_along(block, axis, distance):
    devices = range(lax.axis_size(axis))
    route = [(i - distance, i) for i in devices if i - distance in devices]
    return lax.ppermute(block, axis, route)


def band_matrix(count, radius):
    rows = jnp.arange(count, dtype=jnp.int32)
    dist = jnp.abs(rows[:, None] - rows[None, :])
    weights = jnp.maximum(radius + 1 - dist, 0).astype(jnp.float32)
    return weights / jnp.sum(weights, axis=1, keepdims=True)


def ahead(field, axis):
    count = field.shape[axis]
    rest = lax.slice_in_dim(field, 1, count, axis=axis)
    return jnp.concatenate([rest, jnp.zeros_like(lax.slice_in_dim(field, 0, 1, axis=axis))], axis)


def behind(field, axis):
    count = field.shape[axis]
    rest = lax.slice_in_dim(field, 0, count - 1, axis=axis)
    return jnp.concatenate([jnp.zeros_like(lax.slice_in_dim(field, 0, 1, axis=axis)), rest], axis)


def update_h(efield, hfield, upper):
    ex, ey, ez = (efield[0], efield[1], efield[2])
    ex_next = jnp.concatenate([ex[1:], upper[0][None]], 0)
    ey_next = jnp.concatenate([ey[1:], upper[1][None]], 0)
    curl_x = ahead(ez, 2) - ez - (ey_next - ey)
    curl_y = ex_next - ex - (ahead(ez, 1) - ez)
    curl_z = ahead(ey, 1) - ey - (ahead(ex, 2) - ex)
    return hfield - DT * jnp.stack([curl_x, curl_y, curl_z])


def update_e(efield, hnext, lower, jnext, permittivity, drive):
    hx, hy, hz = (hnext[0], hnext[1], hnext[2])
    hx_prev = jnp.concatenate([lower[0][None], hx[:-1]], 0)
    hy_prev = jnp.concatenate([lower[1][None], hy[:-1]], 0)
    curl_x = hz - behind(hz, 2) - (hy - hy_prev)
    curl_y = hx - hx_prev - (hz - behind(hz, 1))
    curl_z = hy - behind(hy, 1) - (hx - behind(hx, 2))
    curl = jnp.stack([curl_x, curl_y, curl_z])
    return efield + (DT / permittivity)[None] * (curl - jnext + drive)


def update_j(jfield, pfield, efield, strength):
    return ((1.0 - DAMPING * DT / 2.0) * jfield + DT * (strength[None] * efield - pfield)) / (
        1.0 + DAMPING * DT / 2.0
    )


def smooth(wx, wy, planes):
    inner = jnp.einsum("ax,zxy->zay", wx, planes, precision=HIGH)
    return jnp.einsum("zay,by->zab", inner, wy, precision=HIGH)


def smooth_adjoint(wx, wy, planes):
    inner = jnp.einsum("ax,zab->zxb", wx, planes, precision=HIGH)
    return jnp.einsum("zxb,by->zxy", inner, wy, precision=HIGH)


def locate(cells, first, depth, width_x, width_y):
    zz = cells // (width_x * width_y)
    rest = cells % (width_x * width_y)
    local = zz - first
    inside = ((local >= 0) & (local < depth)).astype(jnp.float32)
    return (jnp.clip(local, 0, depth - 1), rest // width_y, rest % width_y, inside)


def body(
    e_forward,
    h_forward,
    p_forward,
    j_forward,
    e_adjoint,
    h_adjoint,
    p_adjoint,
    j_adjoint,
    design,
    source_amp,
    source_cell,
    monitor_cell,
    slab_start,
    radius,
):
    index = lax.axis_index("gx")
    depth, width_x, width_y = (e_forward.shape[1], e_forward.shape[2], e_forward.shape[3])
    start = slab_start[0]
    wx = band_matrix(width_x, radius[0])
    wy = band_matrix(width_y, radius[0])
    upper = passed_along(
        jnp.stack([e_forward[0, 0], e_forward[1, 0], e_adjoint[0, 0], e_adjoint[1, 0]]), "gx", -1
    )
    hf = update_h(e_forward, h_forward, upper[0:2])
    ha = update_h(e_adjoint, h_adjoint, upper[2:4])
    gathered = lax.all_gather(design, "gx", axis=0, tiled=True)
    slab = gathered.shape[0]
    planes = index * depth + jnp.arange(depth, dtype=jnp.int32) - start
    valid = ((planes >= 0) & (planes < slab)).astype(jnp.float32)
    picked = jnp.take(gathered, jnp.clip(planes, 0, slab - 1), axis=0) * valid[:, None, None]
    density = smooth(wx, wy, picked)
    permittivity = 1.0 + EPS_RANGE * density
    strength = STRENGTH_BASE + STRENGTH_RANGE * density
    lower = passed_along(jnp.stack([hf[0, -1], hf[1, -1], ha[0, -1], ha[1, -1]]), "gx", 1)
    zs, xs, ys, inside_s = locate(source_cell, index * depth, depth, width_x, width_y)
    nsrc = zs.shape[0]
    comp = jnp.repeat(jnp.arange(3, dtype=jnp.int32), nsrc)
    drive = (
        jnp.zeros((3, depth, width_x, width_y), jnp.float32)
        .at[comp, jnp.tile(zs, 3), jnp.tile(xs, 3), jnp.tile(ys, 3)]
        .add((source_amp.T * inside_s[None, :]).reshape(-1))
    )
    zm, xm, ym, inside_m = locate(monitor_cell, index * depth, depth, width_x, width_y)
    count = jnp.zeros((depth, width_x, width_y), jnp.float32).at[zm, xm, ym].add(inside_m)
    drive_adj = count[None] * e_forward
    jf = update_j(j_forward, p_forward, e_forward, strength)
    ja = update_j(j_adjoint, p_adjoint, e_adjoint, strength)
    ef = update_e(e_forward, hf, lower[0:2], jf, permittivity, drive)
    ea = update_e(e_adjoint, ha, lower[2:4], ja, permittivity, drive_adj)
    intersection = jnp.sum(ea * (ef - e_forward + GAIN_FIELD * ef), axis=0)
    slots = jnp.arange(slab, dtype=jnp.int32)
    select = (planes[:, None] == slots[None, :]).astype(jnp.float32)
    returned = jnp.einsum("lo,lxy->oxy", select, intersection, precision=HIGH)
    own_intersection = lax.psum_scatter(returned, "gx", scatter_dimension=0, tiled=True)
    design_grad = smooth_adjoint(wx, wy, own_intersection)
    return (ef, hf, ea, ha, design_grad)


def solution(mesh):
    return jax.shard_map(
        body,
        mesh=mesh,
        in_specs=(
            P(None, ("grp", "gx"), None, None),
            P(None, ("grp", "gx"), None, None),
            P(None, ("grp", "gx"), None, None),
            P(None, ("grp", "gx"), None, None),
            P(None, ("grp", "gx"), None, None),
            P(None, ("grp", "gx"), None, None),
            P(None, ("grp", "gx"), None, None),
            P(None, ("grp", "gx"), None, None),
            P(("grp", "gx"), None, None),
            P("grp", None),
            P("grp"),
            P("grp"),
            P("grp"),
            P("grp"),
        ),
        out_specs=(
            P(None, ("grp", "gx"), None, None),
            P(None, ("grp", "gx"), None, None),
            P(None, ("grp", "gx"), None, None),
            P(None, ("grp", "gx"), None, None),
            P(("grp", "gx"), None, None),
        ),
        check_vma=False,
    )
```

profile of v0, /device:TPU:0, one launch (start us, length us, event | category | flops | bytes accessed | tf_op | source)
XLA Modules:
  0.0 142.5 jit_solution(9310592674110908171)
XLA Ops:
  7.2 0.9 slice_bitcast_fusion.25
  8.1 0.7 pad_maximum_fusion
  8.8 1.3 collective-permute-start
  10.7 0.7 convert_reduce_fusion.1
  11.4 0.7 convert_reduce_fusion
  12.1 1.9 %slice_bitcast_fusion.17 = (f32[7,32,256]{2,1,0:T(8,128)}, f32[7,32,256]{2,1,0:T(8,128)}) fusion(f32[3,8,32,256]{3,2,1,0:T(8,128)} %param.18), kind=kLoop, calls=%fused_computation.73 | loop fusion | bytes 917504 | tf_op jit(solution)/shard_map/slice | solution.py:43
  14.0 0.8 slice_bitcast_fusion.19
  14.9 0.1 slice.280
  15.0 0.8 slice_bitcast_fusion.11
  15.8 0.7 slice.272
  16.6 0.8 slice.269
  18.1 0.5 compare_and_fusion
  18.6 0.6 copy-done.28
  19.2 0.5 and_convert_fusion.2
  19.7 0.7 reshape.193
  20.5 0.6 tile.32
  21.1 0.6 tile.30
  21.7 0.6 tile.13
  22.3 0.1 copy-done.27
  22.4 0.1 reshape.207
  22.5 25.4 %all_gather.3 = f32[16,32,256]{2,1,0:T(8,128)S(1)} all-gather(f32[1,32,256]{2,1,0:T(8,128)} %param.22), channel_id=1, replica_groups=mesh['grp'=2,'gx'=16] {'gx'}, dimensions={0}, use_global_device_ids=true | all-gather | bytes 557056 | tf_op jit(solution)/shard_map/all_gather | solution.py:111
  47.9 0.7 slice.284
  48.6 0.1 slice.285
  48.7 0.8 copy-done.11
  49.6 0.8 slice.274
  50.4 0.7 slice.273
  51.1 0.6 gather_fusion
  51.7 0.6 copy-done.30
  52.4 0.4 convolution_bitcast_fusion
  52.8 0.2 copy-done.36
  53.1 1.3 add_divide_fusion
  54.5 1.6 %scatter_fusion.1 = f32[8,32,256]{2,1,0:T(8,128)S(1)} fusion(f32[8,32,256]{2,1,0:T(8,128)S(1)} %broadcast_in_dim.23, s32[16]{0:T(128)S(1)} %fusion.56, f32[16]{0:T(128)S(1)} %get-tuple-element.8), kind=kCustom, calls=%fused_computation.2 | custom fusion | flops 16 | bytes 384 | tf_op jit(solution)/shard_map/scatter-add | solution.py:129
  56.1 0.9 copy-done.10
  57.0 0.2 fusion.10
  57.2 0.9 copy-done.20
  58.1 0.1 fusion.1
  58.3 0.9 slice_bitcast_fusion.13
  59.2 0.9 slice_bitcast_fusion.2
  60.2 0.3 copy-done.7
  60.5 0.1 copy-done.8
  60.6 0.1 copy-done.9
  60.7 0.1 copy-done.12
  60.7 0.1 copy-done.13
  60.8 0.2 fusion.6
  61.0 0.9 copy-done.21
  62.0 0.1 fusion
  62.1 0.1 slice_bitcast_fusion.5
  62.2 2.3 %collective-permute-start.1 = (f32[4,32,256]{2,1,0:T(8,128)S(1)}, f32[4,32,256]{2,1,0:T(8,128)S(1)}, u32[]{:S(2)}, u32[]{:S(2)}) collective-permute-start(f32[4,32,256]{2,1,0:T(8,128)S(1)} %pad_maximum_fusion.1), channel_id=1, source_target_pairs={{0,1},{1,2},{2,3},{3,4},{4,5},{5,6},{6,7},{7,8},{8,9},{9,10},{10,1... | collective-permute-start | bytes 393224 | tf_op jit(solution)/shard_map/ppermute | solution.py:18
  64.5 0.9 collective-permute-done.1
  65.5 0.4 fusion.14
  65.8 0.6 copy-done.4
  66.4 0.3 copy-done.16
  66.7 0.2 copy-done.17
  66.9 0.3 maximum_subtract_fusion
  67.3 4.2 %scatter_fusion = f32[3,8,32,256]{3,2,1,0:T(8,128)S(1)} fusion(f32[3,8,32,256]{3,2,1,0:T(8,128)S(1)} %maximum_subtract_fusion, s32[48]{0:T(128)S(1)} %fusion.59, f32[48]{0:T(128)S(1)} %reshape.207), kind=kCustom, calls=%fused_computation.1 | custom fusion | flops 48 | bytes 1344 | tf_op jit(solution)/shard_map/scatter-add | solution.py:126
  71.5 1.7 %fusion.18 = (f32[1,8,32,256]{3,2,1,0:T(8,128)S(1)}, f32[1,8,32,256]{3,2,1,0:T(8,128)S(1)}, f32[1,8,32,256]{3,2,1,0:T(8,128)S(1)}) fusion(f32[7,32,256]{2,1,0:T(8,128)} %get-tuple-element.28, f32[1,32,256]{2,1,0:T(8,128)S(1)} %get-tuple-element.61, f32[8,32,255]{2,1,0:T(8,128)} %bitcast.192, f32[3,8,32,256]{3,2,1,0:T(8,128)S(1)} %fusion.1, ...), kind=kLoop, calls=%fused_computation.43 | loop fusion | flops 720896 | bytes 3127296 | tf_op jit(solution)/shard_map/stack | solution.py:57
  73.3 0.2 copy-done.19
  73.5 1.8 %multiply_reduce_fusion = (f32[8,32,256]{2,1,0:T(8,128)S(1)}, f32[3,8,32,256]{3,2,1,0:T(8,128)}, f32[3,8,32,256]{3,2,1,0:T(8,128)}) fusion(f32[3,8,32,256]{3,2,1,0:T(8,128)S(1)} %copy-done, f32[3,8,32,256]{3,2,1,0:T(8,128)S(1)} %copy-done.1, f32[8,32,256]{2,1,0:T(8,128)S(1)} %scatter_fusion.1, f32[3,8,32,256]{3,2,1,0:T(8,128)S(1)} %copy-done.18, ...), kind=kLoop, calls=%fused_computation.15 | loop fusion | flops 3866624 | bytes 7340032 | tf_op jit(solution)/shard_map/reduce_sum | solution.py:135
  75.3 0.7 copy-done.29
  76.0 0.5 fusion.23
  76.5 1.1 copy.22
  77.7 55.9 %reduce-scatter.2.cloned.1.call-done = f32[1,32,256]{2,1,0:T(8,128)} async-done(((f32[16,32,256]{2,1,0:T(8,128)}), f32[1,32,256]{2,1,0:T(8,128)}) %reduce-scatter.2.cloned.1.call-update) | async-done | bytes 32784 | tf_op jit(solution)/shard_map/reduce_scatter | solution.py:139
  133.6 1.0 convolution_bitcast_fusion.2
  134.7 0.9 convolution_bitcast_fusion.1
  (83 shorter events, 0.5 us)
Async XLA Ops:
  7.2 6.9 %copy-start = (f32[3,8,32,256]{3,2,1,0:T(8,128)S(1)}, f32[3,8,32,256]{3,2,1,0:T(8,128)}, u32[]{:S(2)}) copy-start(f32[3,8,32,256]{3,2,1,0:T(8,128)} %param.14) | copy-start | bytes 2359300
  7.2 126.4 %reduce-scatter.2.cloned.1.call-start = ((), (), s32[]{:S(2)}) async-start(), calls=%async_computation.1 | async-start | bytes 557056 | tf_op jit(solution)/shard_map/reduce_scatter | solution.py:139
  8.8 47.3 %collective-permute-start = (f32[4,32,256]{2,1,0:T(8,128)}, f32[4,32,256]{2,1,0:T(8,128)S(1)}, u32[]{:S(2)}, u32[]{:S(2)}) collective-permute-start(f32[4,32,256]{2,1,0:T(8,128)} %pad_maximum_fusion), channel_id=1, source_target_pairs={{1,0},{2,1},{3,2},{4,3},{5,4},{6,5},{7,6},{8,7},{9,8},{10,9},{11,1... | collective-permute-start | bytes 393224 | tf_op jit(solution)/shard_map/ppermute | solution.py:18
  12.1 2.7 %copy-start.1 = (f32[3,8,32,256]{3,2,1,0:T(8,128)S(1)}, f32[3,8,32,256]{3,2,1,0:T(8,128)}, u32[]{:S(2)}) copy-start(f32[3,8,32,256]{3,2,1,0:T(8,128)} %param.18) | copy-start | bytes 2359300
  18.6 0.6 copy-start.28
  19.7 0.7 copy-start.31
  19.7 0.7 copy-start.32
  21.7 0.7 copy-start.27
  48.6 0.9 copy-start.11
  51.7 0.7 copy-start.30
  51.7 0.6 copy-start.33
  51.7 0.7 copy-start.35
  52.4 0.7 copy-start.36
  54.4 1.6 %copy-start.23 = (s32[48,1]{0,1:T(1,128)S(1)}, s32[48,1]{0,1:T(1,128)}, u32[]{:S(2)}) copy-start(s32[48,1]{0,1:T(1,128)} %reshape.193) | copy-start | bytes 580
  54.4 1.6 %copy-start.24 = (s32[48,1]{0,1:T(1,128)S(1)}, s32[48,1]{0,1:T(1,128)}, u32[]{:S(2)}) copy-start(s32[48,1]{0,1:T(1,128)} %tile.32) | copy-start | bytes 580
  54.4 1.6 %copy-start.25 = (s32[48,1]{0,1:T(1,128)S(1)}, s32[48,1]{0,1:T(1,128)}, u32[]{:S(2)}) copy-start(s32[48,1]{0,1:T(1,128)} %tile.30) | copy-start | bytes 580
  54.4 1.6 %copy-start.26 = (s32[48,1]{0,1:T(1,128)S(1)}, s32[48,1]{0,1:T(1,128)}, u32[]{:S(2)}) copy-start(s32[48,1]{0,1:T(1,128)} %tile.13) | copy-start | bytes 580
  54.4 1.7 %copy-start.14 = (f32[7,32,256]{2,1,0:T(8,128)S(1)}, f32[7,32,256]{2,1,0:T(8,128)}, u32[]{:S(2)}) copy-start(f32[7,32,256]{2,1,0:T(8,128)} %get-tuple-element.48) | copy-start | bytes 688132
  54.4 1.7 %copy-start.15 = (f32[7,32,256]{2,1,0:T(8,128)S(1)}, f32[7,32,256]{2,1,0:T(8,128)}, u32[]{:S(2)}) copy-start(f32[7,32,256]{2,1,0:T(8,128)} %get-tuple-element.49) | copy-start | bytes 688132
  56.1 1.0 copy-start.10
  57.0 1.1 copy-start.20
  58.3 13.2 %copy-start.2 = (f32[3,8,32,256]{3,2,1,0:T(8,128)}, f32[3,8,32,256]{3,2,1,0:T(8,128)S(1)}, u32[]{:S(2)}) copy-start(f32[3,8,32,256]{3,2,1,0:T(8,128)S(1)} %fusion.1) | copy-start | bytes 2359300
  59.2 1.0 copy-start.6
  59.2 1.2 copy-start.7
  59.2 1.4 copy-start.8
  59.2 1.5 %copy-start.9 = (f32[8,31,256]{2,1,0:T(8,128)S(1)}, f32[8,31,256]{2,1,0:T(8,128)}, u32[]{:S(2)}) copy-start(f32[8,31,256]{2,1,0:T(8,128)} %slice.273) | copy-start | bytes 761860
  59.2 1.5 %copy-start.12 = (f32[7,32,256]{2,1,0:T(8,128)S(1)}, f32[7,32,256]{2,1,0:T(8,128)}, u32[]{:S(2)}) copy-start(f32[7,32,256]{2,1,0:T(8,128)} %get-tuple-element.38) | copy-start | bytes 688132
  59.2 1.6 %copy-start.13 = (f32[7,32,256]{2,1,0:T(8,128)S(1)}, f32[7,32,256]{2,1,0:T(8,128)}, u32[]{:S(2)}) copy-start(f32[7,32,256]{2,1,0:T(8,128)} %get-tuple-element.39) | copy-start | bytes 688132
  60.8 1.1 copy-start.21
  62.1 3.4 %copy-start.3 = (f32[3,8,32,256]{3,2,1,0:T(8,128)}, f32[3,8,32,256]{3,2,1,0:T(8,128)S(1)}, u32[]{:S(2)}) copy-start(f32[3,8,32,256]{3,2,1,0:T(8,128)S(1)} %fusion) | copy-start | bytes 2359300
  62.2 3.2 %collective-permute-start.1 = (f32[4,32,256]{2,1,0:T(8,128)S(1)}, f32[4,32,256]{2,1,0:T(8,128)S(1)}, u32[]{:S(2)}, u32[]{:S(2)}) collective-permute-start(f32[4,32,256]{2,1,0:T(8,128)S(1)} %pad_maximum_fusion.1), channel_id=1, source_target_pairs={{0,1},{1,2},{2,3},{3,4},{4,5},{5,6},{6,7},{7,8},{8,9},{9,10},{10,1... | collective-permute-start | bytes 393224 | tf_op jit(solution)/shard_map/ppermute | solution.py:18
  65.4 1.0 copy-start.4
  65.5 1.2 copy-start.16
  65.5 1.4 %copy-start.17 = (f32[3,8,32,256]{3,2,1,0:T(8,128)S(1)}, f32[3,8,32,256]{3,2,1,0:T(8,128)}, u32[]{:S(2)}) copy-start(f32[3,8,32,256]{3,2,1,0:T(8,128)} %param.17) | copy-start | bytes 2359300
  71.5 1.8 %copy-start.5 = (f32[8,32,256]{2,1,0:T(8,128)S(1)}, f32[8,32,256]{2,1,0:T(8,128)}, u32[]{:S(2)}) copy-start(f32[8,32,256]{2,1,0:T(8,128)} %get-tuple-element.58) | copy-start | bytes 786436
  71.5 1.8 %copy-start.18 = (f32[3,8,32,256]{3,2,1,0:T(8,128)S(1)}, f32[3,8,32,256]{3,2,1,0:T(8,128)}, u32[]{:S(2)}) copy-start(f32[3,8,32,256]{3,2,1,0:T(8,128)} %param.20) | copy-start | bytes 2359300
  71.5 1.9 %copy-start.19 = (f32[3,8,32,256]{3,2,1,0:T(8,128)S(1)}, f32[3,8,32,256]{3,2,1,0:T(8,128)}, u32[]{:S(2)}) copy-start(f32[3,8,32,256]{3,2,1,0:T(8,128)} %param.21) | copy-start | bytes 2359300
  71.5 2.0 %copy-start.22 = (f32[8,32,256]{2,1,0:T(8,128)S(1)}, f32[8,32,256]{2,1,0:T(8,128)}, u32[]{:S(2)}) copy-start(f32[8,32,256]{2,1,0:T(8,128)} %get-tuple-element.57) | copy-start | bytes 786436
  75.3 0.7 copy-start.29
  77.6 56.0 %copy-start.34 = (f32[32]{0:T(128)S(1)}, f32[32]{0:T(128)}, u32[]{:S(2)}) copy-start(f32[32]{0:T(128)} %convert_reduce_fusion.1) | copy-start | bytes 388
  77.6 57.0 %copy-start.37 = (f32[256]{0:T(256)S(1)}, f32[256]{0:T(256)}, u32[]{:S(2)}) copy-start(f32[256]{0:T(256)} %convert_reduce_fusion) | copy-start | bytes 3076
Sparse Core Ops, SparseCore 0:
  77.8 55.7 reduce-scatter.1
where the time goes:
time: 143 us; the launch traced here: 142 us
  waiting for transfers between devices  56.9 us (40%)
  blocking collectives  25.4 us (18%)
  local copies, waits for them, and re-layouts  22.6 us (16%)
  between operations  15.9 us (11%)
  other arithmetic  13.9 us (10%)
  matrix products  4.26 us (3%)
  starting transfers between devices  3.57 us (2%)
    reduce_scatter x1, waiting for transfers between devices, body(): lax.psum_scatter(returned, 'gx', scatter_dimension=0, tiled=True)  55.9 us
    all_gather x1, blocking collectives, body(): gathered = lax.all_gather(design, 'gx', axis=0, tiled=True)  25.4 us
    unnamed x76, local copies, waits for them, and re-layouts  7.77 us
    scatter-add x1, other arithmetic, body(): drive = jnp.zeros((3, depth, width_x, width_y), jnp.float32).at[comp, jnp...  4.22 us
    slice x8, local copies, waits for them, and re-layouts, ahead(): rest = lax.slice_in_dim(field, 1, count, axis=axis)  4.17 us
    ppermute x2, starting transfers between devices, passed_along(): return lax.ppermute(block, axis, route)  3.53 us
  transfers between devices with their start and end apart: 3, of which 2 were waited for; matrix products, arithmetic and copies ran while one was open for 12% of the time, Pallas kernels for 0%

commit v1 on v0

--- a/solution.py
+++ b/solution.py
@@ -1,3 +1,4 @@
+import functools
 import jax
 import jax.numpy as jnp
 from jax import lax
@@ -10,6 +11,27 @@
 DAMPING = 0.2
 GAIN_FIELD = 0.25
 HIGH = lax.Precision.HIGHEST
+
+
+def draw_types_all(xx, lane_axis):
+    spare, met_up, w1 = (lax.psum(1, lane_axis), lax.axis_index(lane_axis), xx.shape[0])
+    z, work_now = (xx, 1)
+    while work_now < spare:
+        z = jnp.concatenate(
+            [
+                z,
+                lax.ppermute(
+                    z, lane_axis, list(map(lambda k0: (k0, (k0 - work_now) % spare), range(spare)))
+                ),
+            ],
+            axis=0,
+        )
+        work_now = 2 * work_now
+    before = jnp.roll(z, met_up * w1, axis=0)
+    return before
+
+
+process_array_by_axis = functools.partial(draw_types_all, lane_axis="gx")
 
 
 def passed_along(block, axis, distance):
@@ -108,7 +130,7 @@
     )
     hf = update_h(e_forward, h_forward, upper[0:2])
     ha = update_h(e_adjoint, h_adjoint, upper[2:4])
-    gathered = lax.all_gather(design, "gx", axis=0, tiled=True)
+    gathered = process_array_by_axis(design)
     slab = gathered.shape[0]
     planes = index * depth + jnp.arange(depth, dtype=jnp.int32) - start
     valid = ((planes >= 0) & (planes < slab)).astype(jnp.float32)

time: 143 us -> 134 us (0.937)
  blocking collectives: 25.4 us -> 0 us
  waiting for transfers between devices: 56.9 us -> 71.2 us
  starting transfers between devices: 3.57 us -> 10.4 us
  local copies, waits for them, and re-layouts: 22.6 us -> 17.3 us
    all_gather x1 -> x0, blocking collectives: 25.4 us -> none  [body(): gathered = lax.all_gather(design, 'gx', axis=0, tiled=True)]
    ppermute x0 -> x4, waiting for transfers between devices: none -> 15.2 us  [draw_types_all(): lax.ppermute(z, lane_axis, list(map(lambda k0: (k0, (k0 - work_now) % spa...]
    ppermute x0 -> x4, starting transfers between devices: none -> 7.56 us  [draw_types_all(): lax.ppermute(z, lane_axis, list(map(lambda k0: (k0, (k0 - work_now) % spa...]
    slice x8, local copies, waits for them, and re-layouts: 4.17 us -> 2.01 us  [ahead(): rest = lax.slice_in_dim(field, 1, count, axis=axis)]
    unnamed x76 -> x63, local copies, waits for them, and re-layouts: 7.77 us -> 7.65 us
  transfers between devices with their start and end apart: 3 -> 7, of which waited for: 2 -> 4; matrix products, arithmetic and copies ran while one was open for 12% -> 11% of each run, Pallas kernels for 0% -> 0%
where the time goes in v1:
time: 134 us; the launch traced here: 133 us
  waiting for transfers between devices  71.2 us (53%)
  local copies, waits for them, and re-layouts  17.3 us (13%)
  between operations  16 us (12%)
  other arithmetic  14.3 us (11%)
  starting transfers between devices  10.4 us (8%)
  matrix products  4.19 us (3%)
    reduce_scatter x1, waiting for transfers between devices, body(): lax.psum_scatter(returned, 'gx', scatter_dimension=0, tiled=True)  55.1 us
    ppermute x4, waiting for transfers between devices, draw_types_all(): lax.ppermute(z, lane_axis, list(map(lambda k0: (k0, (k0 - work_now) % spa...  15.2 us
    unnamed x63, local copies, waits for them, and re-layouts  7.65 us
    ppermute x4, starting transfers between devices, draw_types_all(): lax.ppermute(z, lane_axis, list(map(lambda k0: (k0, (k0 - work_now) % spa...  7.56 us
    scatter-add x1, other arithmetic, body(): drive = jnp.zeros((3, depth, width_x, width_y), jnp.float32).at[comp, jnp...  4.22 us
    reduce_sum x1, other arithmetic, body(): intersection = jnp.sum(ea * (ef - e_forward + GAIN_FIELD * ef), axis=0)  3.25 us
    ppermute x2, starting transfers between devices, passed_along(): return lax.ppermute(block, axis, route)  2.84 us
  transfers between devices with their start and end apart: 7, of which 4 were waited for; matrix products, arithmetic and copies ran while one was open for 11% of the time, Pallas kernels for 0%

profile of v1, /device:TPU:0, one launch (start us, length us, event | category | flops | bytes accessed | tf_op | source)
XLA Modules:
  0.0 133.4 jit_solution(16941229090689174029)
XLA Ops:
  7.2 0.0 reduce-scatter.2.cloned.1.call-start
  7.2 0.8 slice_bitcast_fusion.25
  8.0 0.7 pad_maximum_fusion.2
  8.7 1.4 %collective-permute-start.4 = (f32[4,32,256]{2,1,0:T(8,128)}, f32[4,32,256]{2,1,0:T(8,128)}, u32[]{:S(2)}, u32[]{:S(2)}) collective-permute-start(f32[4,32,256]{2,1,0:T(8,128)} %pad_maximum_fusion.2), channel_id=1, source_target_pairs={{1,0},{2,1},{3,2},{4,3},{5,4},{6,5},{7,6},{8,7},{9,8},{10,9},{11,1... | collective-permute-start | bytes 393224 | tf_op jit(solution)/shard_map/ppermute | solution.py:40
  10.1 7.4 %collective-permute-start = (f32[1,32,256]{2,1,0:T(8,128)S(1)}, f32[1,32,256]{2,1,0:T(8,128)S(1)}, u32[]{:S(2)}, u32[]{:S(2)}) collective-permute-start(f32[1,32,256]{2,1,0:T(8,128)S(1)} %copy-done.18), channel_id=1, source_target_pairs={{0,15},{1,0},{2,1},{3,2},{4,3},{5,4},{6,5},{7,6},{8,7},{9,8},{10,9... | collective-permute-start | bytes 98312 | tf_op jit(solution)/shard_map/ppermute | solution.py:23
  17.5 1.2 slice_bitcast_fusion.11
  18.7 0.8 slice_bitcast_fusion.19
  19.5 0.5 copy-done.1
  20.0 0.8 slice_bitcast_fusion.8
  20.8 0.8 slice_bitcast_fusion.17
  21.6 0.6 constant_dynamic-update-slice_fusion.9
  22.9 0.6 copy-done.25
  23.6 0.0 copy-done.26
  23.6 0.1 tile.32
  23.7 0.1 tile.30
  23.8 0.1 tile.13
  23.9 0.1 reshape.193
  24.0 0.7 copy-done.24
  24.7 0.1 slice.269
  24.9 0.1 slice.280
  25.1 0.7 slice.273
  25.8 0.8 slice.274
  26.6 0.1 copy-done.14
  26.8 0.9 copy-done.13
  27.7 0.1 slice.285
  28.5 0.1 reshape.207
  28.6 1.6 %scatter_fusion.1 = f32[8,32,256]{2,1,0:T(8,128)S(1)} fusion(f32[8,32,256]{2,1,0:T(8,128)S(1)} %broadcast_in_dim.23, s32[16]{0:T(128)S(1)} %fusion.56, f32[16]{0:T(128)S(1)} %get-tuple-element.8), kind=kCustom, calls=%fused_computation.2 | custom fusion | flops 16 | bytes 384 | tf_op jit(solution)/shard_map/scatter-add | solution.py:151
  30.2 0.1 convert_reduce_fusion.1
  30.3 0.2 convert_reduce_fusion
  30.5 0.1 collective-permute-start.1
  30.5 0.6 constant_dynamic-update-slice_fusion.8
  31.1 3.6 %collective-permute-done.1 = f32[2,32,256]{2,1,0:T(8,128)S(1)} collective-permute-done((f32[2,32,256]{2,1,0:T(8,128)S(1)}, f32[2,32,256]{2,1,0:T(8,128)S(1)}, u32[]{:S(2)}, u32[]{:S(2)}) %collective-permute-start.1) | collective-permute-done | bytes 65568 | tf_op jit(solution)/shard_map/ppermute | solution.py:23
  34.8 0.1 collective-permute-start.2
  34.9 0.6 constant_dynamic-update-slice_fusion.7
  35.5 0.8 fusion.69
  36.4 1.2 fusion.6
  37.6 0.0 copy-done.21
  37.6 0.1 fusion
  37.7 0.1 slice_bitcast_fusion.5
  37.9 1.1 copy-done.15
  39.0 0.1 copy-done.16
  39.1 0.2 fusion.10
  39.3 0.9 copy-done.22
  40.2 0.1 fusion.1
  40.3 0.1 slice_bitcast_fusion.2
  40.4 1.4 %collective-permute-start.5 = (f32[4,32,256]{2,1,0:T(8,128)S(1)}, f32[4,32,256]{2,1,0:T(8,128)S(1)}, u32[]{:S(2)}, u32[]{:S(2)}) collective-permute-start(f32[4,32,256]{2,1,0:T(8,128)S(1)} %pad_maximum_fusion.3), channel_id=1, source_target_pairs={{0,1},{1,2},{2,3},{3,4},{4,5},{5,6},{6,7},{7,8},{8,9},{9,10},{10,1... | collective-permute-start | bytes 393224 | tf_op jit(solution)/shard_map/ppermute | solution.py:40
  42.0 0.1 collective-permute-start.3
  42.1 0.8 collective-permute-done.5
  42.9 1.1 fusion.14
  44.0 1.1 fusion.18
  45.1 11.6 %collective-permute-done.3 = f32[8,32,256]{2,1,0:T(8,128)S(1)} collective-permute-done((f32[8,32,256]{2,1,0:T(8,128)S(1)}, f32[8,32,256]{2,1,0:T(8,128)S(1)}, u32[]{:S(2)}, u32[]{:S(2)}) %collective-permute-start.3) | collective-permute-done | bytes 262176 | tf_op jit(solution)/shard_map/ppermute | solution.py:23
  56.8 0.6 gather_fusion
  57.4 0.4 convolution_bitcast_fusion
  57.9 1.2 add_divide_fusion
  59.2 0.7 copy-done.10
  59.9 0.3 maximum_subtract_fusion
  60.3 4.2 %scatter_fusion = f32[3,8,32,256]{3,2,1,0:T(8,128)S(1)} fusion(f32[3,8,32,256]{3,2,1,0:T(8,128)S(1)} %maximum_subtract_fusion, s32[48]{0:T(128)S(1)} %fusion.59, f32[48]{0:T(128)S(1)} %reshape.207), kind=kCustom, calls=%fused_computation.1 | custom fusion | flops 48 | bytes 1344 | tf_op jit(solution)/shard_map/scatter-add | solution.py:148
  64.5 3.3 %multiply_reduce_fusion = (f32[8,32,256]{2,1,0:T(8,128)S(1)}, f32[3,8,32,256]{3,2,1,0:T(8,128)}, f32[3,8,32,256]{3,2,1,0:T(8,128)}) fusion(f32[3,8,32,256]{3,2,1,0:T(8,128)S(1)} %copy-done, f32[3,8,32,256]{3,2,1,0:T(8,128)S(1)} %copy-done.1, f32[8,32,256]{2,1,0:T(8,128)S(1)} %scatter_fusion.1, f32[3,8,32,256]{3,2,1,0:T(8,128)} %param.20, ...), kind=kLoop, calls=%fused_computation.15 | loop fusion | flops 3866624 | bytes 7340032 | tf_op jit(solution)/shard_map/reduce_sum | solution.py:157
  67.8 0.5 fusion.23
  68.3 1.1 copy.22
  69.4 0.0 reduce-scatter.2.cloned.1.call-update
  69.4 55.1 %reduce-scatter.2.cloned.1.call-done = f32[1,32,256]{2,1,0:T(8,128)} async-done(((f32[16,32,256]{2,1,0:T(8,128)}), f32[1,32,256]{2,1,0:T(8,128)}) %reduce-scatter.2.cloned.1.call-update) | async-done | bytes 32784 | tf_op jit(solution)/shard_map/reduce_scatter | solution.py:161
  124.6 1.0 convolution_bitcast_fusion.2
  125.6 0.9 convolution_bitcast_fusion.1
  (82 shorter events, 0.6 us)
Async XLA Ops:
  7.2 117.4 %reduce-scatter.2.cloned.1.call-start = ((), (), s32[]{:S(2)}) async-start(), calls=%async_computation.1 | async-start | bytes 557056 | tf_op jit(solution)/shard_map/reduce_scatter | solution.py:161
  8.0 2.1 %copy-start.18 = (f32[1,32,256]{2,1,0:T(8,128)S(1)}, f32[1,32,256]{2,1,0:T(8,128)}, u32[]{:S(2)}) copy-start(f32[1,32,256]{2,1,0:T(8,128)} %param.22) | copy-start | bytes 98308
  8.7 10.0 %copy-start = (f32[3,8,32,256]{3,2,1,0:T(8,128)S(1)}, f32[3,8,32,256]{3,2,1,0:T(8,128)}, u32[]{:S(2)}) copy-start(f32[3,8,32,256]{3,2,1,0:T(8,128)} %param.14) | copy-start | bytes 2359300
  8.7 26.8 %collective-permute-start.4 = (f32[4,32,256]{2,1,0:T(8,128)}, f32[4,32,256]{2,1,0:T(8,128)}, u32[]{:S(2)}, u32[]{:S(2)}) collective-permute-start(f32[4,32,256]{2,1,0:T(8,128)} %pad_maximum_fusion.2), channel_id=1, source_target_pairs={{1,0},{2,1},{3,2},{4,3},{5,4},{6,5},{7,6},{8,7},{9,8},{10,9},{11,1... | collective-permute-start | bytes 393224 | tf_op jit(solution)/shard_map/ppermute | solution.py:40
  10.1 20.3 %collective-permute-start = (f32[1,32,256]{2,1,0:T(8,128)S(1)}, f32[1,32,256]{2,1,0:T(8,128)S(1)}, u32[]{:S(2)}, u32[]{:S(2)}) collective-permute-start(f32[1,32,256]{2,1,0:T(8,128)S(1)} %copy-done.18), channel_id=1, source_target_pairs={{0,15},{1,0},{2,1},{3,2},{4,3},{5,4},{6,5},{7,6},{8,7},{9,8},{10,9... | collective-permute-start | bytes 98312 | tf_op jit(solution)/shard_map/ppermute | solution.py:23
  18.7 1.3 copy-start.1
  22.9 0.7 copy-start.25
  22.9 0.7 copy-start.26
  24.0 0.7 copy-start.24
  25.8 0.9 copy-start.14
  26.7 0.9 copy-start.13
  30.4 5.9 %copy-start.17 = (f32[7,32,256]{2,1,0:T(8,128)S(1)}, f32[7,32,256]{2,1,0:T(8,128)}, u32[]{:S(2)}) copy-start(f32[7,32,256]{2,1,0:T(8,128)} %get-tuple-element.38) | copy-start | bytes 688132
  30.5 4.3 %collective-permute-start.1 = (f32[2,32,256]{2,1,0:T(8,128)S(1)}, f32[2,32,256]{2,1,0:T(8,128)S(1)}, u32[]{:S(2)}, u32[]{:S(2)}) collective-permute-start(f32[2,32,256]{2,1,0:T(8,128)S(1)} %pad_maximum_fusion.4), channel_id=1, source_target_pairs={{0,14},{1,15},{2,0},{3,1},{4,2},{5,3},{6,4},{7,5},{8,6},{9,7},{10,... | collective-permute-start | bytes 196616 | tf_op jit(solution)/shard_map/ppermute | solution.py:23
  34.8 1.6 %copy-start.12 = (f32[8,32,255]{2,1,0:T(8,128)S(1)}, f32[8,32,255]{2,1,0:T(8,128)}, u32[]{:S(2)}) copy-start(f32[8,32,255]{2,1,0:T(8,128)} %slice.274) | copy-start | bytes 783364
  34.8 1.6 %copy-start.11 = (f32[8,31,256]{2,1,0:T(8,128)S(1)}, f32[8,31,256]{2,1,0:T(8,128)}, u32[]{:S(2)}) copy-start(f32[8,31,256]{2,1,0:T(8,128)} %slice.273) | copy-start | bytes 761860
  34.8 7.1 %collective-permute-start.2 = (f32[4,32,256]{2,1,0:T(8,128)S(1)}, f32[4,32,256]{2,1,0:T(8,128)S(1)}, u32[]{:S(2)}, u32[]{:S(2)}) collective-permute-start(f32[4,32,256]{2,1,0:T(8,128)S(1)} %pad_maximum_fusion.1), channel_id=1, source_target_pairs={{0,12},{1,13},{2,14},{3,15},{4,0},{5,1},{6,2},{7,3},{8,4},{9,5},{1... | collective-permute-start | bytes 393224 | tf_op jit(solution)/shard_map/ppermute | solution.py:23
  36.4 1.2 copy-start.21
  37.7 5.1 %copy-start.2 = (f32[3,8,32,256]{3,2,1,0:T(8,128)}, f32[3,8,32,256]{3,2,1,0:T(8,128)S(1)}, u32[]{:S(2)}) copy-start(f32[3,8,32,256]{3,2,1,0:T(8,128)S(1)} %fusion) | copy-start | bytes 2359300
  37.8 1.2 copy-start.15
  37.8 1.3 copy-start.16
  39.1 1.1 copy-start.22
  40.3 3.7 %copy-start.3 = (f32[3,8,32,256]{3,2,1,0:T(8,128)}, f32[3,8,32,256]{3,2,1,0:T(8,128)S(1)}, u32[]{:S(2)}) copy-start(f32[3,8,32,256]{3,2,1,0:T(8,128)S(1)} %fusion.1) | copy-start | bytes 2359300
  40.4 1.6 %copy-start.23 = (f32[32,32,256]{2,1,0:T(8,128)S(1)}, f32[32,32,256]{2,1,0:T(8,128)}, u32[]{:S(2)}) copy-start(f32[32,32,256]{2,1,0:T(8,128)} %constant_dynamic-update-slice_fusion.7) | copy-start | bytes 3145732
  40.4 2.4 %collective-permute-start.5 = (f32[4,32,256]{2,1,0:T(8,128)S(1)}, f32[4,32,256]{2,1,0:T(8,128)S(1)}, u32[]{:S(2)}, u32[]{:S(2)}) collective-permute-start(f32[4,32,256]{2,1,0:T(8,128)S(1)} %pad_maximum_fusion.3), channel_id=1, source_target_pairs={{0,1},{1,2},{2,3},{3,4},{4,5},{5,6},{6,7},{7,8},{8,9},{9,10},{10,1... | collective-permute-start | bytes 393224 | tf_op jit(solution)/shard_map/ppermute | solution.py:40
  42.0 14.7 %collective-permute-start.3 = (f32[8,32,256]{2,1,0:T(8,128)S(1)}, f32[8,32,256]{2,1,0:T(8,128)S(1)}, u32[]{:S(2)}, u32[]{:S(2)}) collective-permute-start(f32[8,32,256]{2,1,0:T(8,128)S(1)} %pad_maximum_fusion), channel_id=1, source_target_pairs={{0,8},{1,9},{2,10},{3,11},{4,12},{5,13},{6,14},{7,15},{8,0},{9,1},... | collective-permute-start | bytes 786440 | tf_op jit(solution)/shard_map/ppermute | solution.py:23
  57.4 2.4 %copy-start.20 = (f32[3,8,32,256]{3,2,1,0:T(8,128)S(1)}, f32[3,8,32,256]{3,2,1,0:T(8,128)}, u32[]{:S(2)}) copy-start(f32[3,8,32,256]{3,2,1,0:T(8,128)} %param.17) | copy-start | bytes 2359300
  57.9 2.0 %copy-start.4 = (f32[1,8,32,256]{3,2,1,0:T(8,128)S(1)}, f32[1,8,32,256]{3,2,1,0:T(8,128)}, u32[]{:S(2)}) copy-start(f32[1,8,32,256]{3,2,1,0:T(8,128)} %get-tuple-element.17) | copy-start | bytes 786436
  57.9 2.0 %copy-start.5 = (f32[1,8,32,256]{3,2,1,0:T(8,128)S(1)}, f32[1,8,32,256]{3,2,1,0:T(8,128)}, u32[]{:S(2)}) copy-start(f32[1,8,32,256]{3,2,1,0:T(8,128)} %get-tuple-element.18) | copy-start | bytes 786436
  57.9 2.0 %copy-start.6 = (f32[1,8,32,256]{3,2,1,0:T(8,128)S(1)}, f32[1,8,32,256]{3,2,1,0:T(8,128)}, u32[]{:S(2)}) copy-start(f32[1,8,32,256]{3,2,1,0:T(8,128)} %get-tuple-element.19) | copy-start | bytes 786436
  57.9 2.0 %copy-start.19 = (f32[3,8,32,256]{3,2,1,0:T(8,128)S(1)}, f32[3,8,32,256]{3,2,1,0:T(8,128)}, u32[]{:S(2)}) copy-start(f32[3,8,32,256]{3,2,1,0:T(8,128)} %param.16) | copy-start | bytes 2359300
  59.2 0.7 copy-start.10
  60.2 4.3 %copy-start.7 = (f32[1,8,32,256]{3,2,1,0:T(8,128)S(1)}, f32[1,8,32,256]{3,2,1,0:T(8,128)}, u32[]{:S(2)}) copy-start(f32[1,8,32,256]{3,2,1,0:T(8,128)} %get-tuple-element.25) | copy-start | bytes 786436
  60.2 4.3 %copy-start.8 = (f32[1,8,32,256]{3,2,1,0:T(8,128)S(1)}, f32[1,8,32,256]{3,2,1,0:T(8,128)}, u32[]{:S(2)}) copy-start(f32[1,8,32,256]{3,2,1,0:T(8,128)} %get-tuple-element.26) | copy-start | bytes 786436
  60.3 4.3 %copy-start.9 = (f32[1,8,32,256]{3,2,1,0:T(8,128)S(1)}, f32[1,8,32,256]{3,2,1,0:T(8,128)}, u32[]{:S(2)}) copy-start(f32[1,8,32,256]{3,2,1,0:T(8,128)} %get-tuple-element.27) | copy-start | bytes 786436
Sparse Core Ops, SparseCore 0:
  69.6 54.9 reduce-scatter.1
